TPU v7x, 256 devices: a whole 4x4x8 slice. The times are simulated.
256 devices in a mesh: gx: 8 (over x, core), gy: 32 (over y, z).
Axes of the slice: x: 4, y: 4, z: 8, core: 2. Of those that a mesh axis runs over, the one named last changes fastest.
Arguments:
- hidden_in: bfloat16 [8192, 4096], P('gx', 'gy')
- norm_gain: bfloat16 [4096], P('gy'), may hold values from 0.099609375 to 1.8984375
- query_proj: bfloat16 [4096, 4096], P('gx', 'gy')
- kv_proj: bfloat16 [1024, 4096], P(None, 'gy')
- prompt_lengths: int32 [8], replicated, may hold values from 1 to 4096, 8192 in all
- cache_slot: int32 [512], replicated, may hold values from 0 to 511, as said below
Outputs:
- attention: bfloat16 [8192, 4096], P('gy', 'gx')
- kv_cache: bfloat16 [512, 16, 1024], P('gy', None, 'gx')
Inputs may be any that keep to these rules, and one draw needn't show every extreme that they name: `prompt_lengths`: the 8 prompts sum to 8192 tokens; the longest has exactly 4096. `cache_slot`: A permutation of the 512 slots; slot s is held by index s // 16 of gy. The 16 pages of one token block go to any one index at most 1 times, and every index receives exactly 16 pages.
All inputs are finite; a program needn't handle non-finite values.
Results may differ from a plain program's by a relative error of at most 0.0066.
The roundings to bfloat16 on the way count: a program that leaves them out, or rounds other values in their place, can miss the bound.
Values may be sent and summed in bfloat16 or wider, within the bound.
No kernel may reach another device: no remote copies, remote signals or barrier semaphores. Data moves between devices by JAX's collectives and lax.ppermute only.
A program may use at most 128 MiB of HBM per device.

v0:
```python
import math
import jax
import jax.numpy as jnp
from jax import lax
from jax.sharding import PartitionSpec as P

D = 4096
H = 32
KVH = 4
HD = 128
PAGES_DEV = 16
epsilon = 1e-06
rope_base = 5000000.0
masked_out = -1e30


def token_places(prompt_lengths, token_index):
    prompt_ends = jnp.cumsum(prompt_lengths)
    prompt_starts = prompt_ends - prompt_lengths
    segment = jnp.sum((token_index[:, None] >= prompt_ends[None, :]).astype(jnp.int32), axis=1)
    chosen = segment[:, None] == jnp.arange(prompt_lengths.shape[0], dtype=jnp.int32)[None, :]
    opening = jnp.sum(jnp.where(chosen, prompt_starts[None, :], 0), axis=1)
    return (segment, token_index - opening)


def rotate(vectors, places):
    half_size = vectors.shape[-1] // 2
    frequency = rope_base ** (-(jnp.arange(half_size, dtype=jnp.float32) * 2.0) / vectors.shape[-1])
    angles = places.astype(jnp.float32)[:, None] * frequency[None, :]
    cos_part = jnp.cos(angles)[:, None, :]
    sin_part = jnp.sin(angles)[:, None, :]
    leading = vectors[..., :half_size]
    trailing = vectors[..., half_size:]
    return jnp.concatenate(
        [leading * cos_part - trailing * sin_part, trailing * cos_part + leading * sin_part],
        axis=-1,
    )


def local(hidden_in, norm_gain, query_proj, kv_proj, prompt_lengths, cache_slot):
    count_gx = lax.axis_size("gx")
    count_gy = lax.axis_size("gy")
    where_gx = lax.axis_index("gx")
    where_gy = lax.axis_index("gy")
    local_rows = hidden_in.shape[0]
    block_tokens = local_rows * count_gx // count_gy
    all_tokens = block_tokens * count_gy
    heads_here = query_proj.shape[0] // HD
    group_size = H // KVH
    kv_head = where_gx * heads_here // group_size
    contract = (((1,), (1,)), ((), ()))
    kv_width = 2 * HD
    kv_start = kv_head * 2 * HD
    kv_rows = lax.dynamic_slice_in_dim(kv_proj, kv_start, kv_width, 0)
    widened = hidden_in.astype(jnp.float32)
    squares = jnp.sum(widened * widened, axis=1)
    totals = lax.psum(squares, "gy")
    normed = (
        widened * lax.rsqrt(totals / D + epsilon)[:, None] * norm_gain.astype(jnp.float32)[None, :]
    ).astype(jnp.bfloat16)
    gathered = lax.all_gather(normed, "gx", axis=0, tiled=True)
    stacked = jnp.concatenate([query_proj, kv_rows], axis=0)
    projected = lax.psum_scatter(
        lax.dot_general(gathered, stacked, contract, preferred_element_type=jnp.float32),
        "gy",
        scatter_dimension=0,
        tiled=True,
    )
    every_index = jnp.arange(all_tokens, dtype=jnp.int32)
    segment_all, place_all = token_places(prompt_lengths, every_index)
    first_query = where_gy * block_tokens
    token_index = first_query + jnp.arange(block_tokens, dtype=jnp.int32)
    segment_own = lax.dynamic_slice_in_dim(segment_all, first_query, block_tokens, 0)
    place_own = lax.dynamic_slice_in_dim(place_all, first_query, block_tokens, 0)
    query_cols = heads_here * HD
    queries = rotate(
        projected[:, :query_cols].reshape(block_tokens, heads_here, HD), place_own
    ).astype(jnp.bfloat16)
    keys = rotate(projected[:, query_cols : query_cols + HD][:, None, :], place_own)[
        :, 0, :
    ].astype(jnp.bfloat16)
    values = projected[:, query_cols + HD :].astype(jnp.bfloat16)
    cache_cols = jnp.where(where_gx % 2 == 0, keys, values)
    score_scale = 1.0 / math.sqrt(HD)
    last_query = first_query + block_tokens - 1
    first_segment = segment_own[0]
    initial = (
        jnp.full((heads_here, block_tokens), masked_out, jnp.float32),
        jnp.zeros((heads_here, block_tokens), jnp.float32),
        jnp.zeros((heads_here, block_tokens, HD), jnp.float32),
    )
    key_piece = lax.all_gather(keys, "gy", axis=0, tiled=True)
    value_piece = lax.all_gather(values, "gy", axis=0, tiled=True)
    block_count = key_piece.shape[0] // block_tokens
    key_blocks = key_piece.reshape(block_count, block_tokens, HD)
    value_blocks = value_piece.reshape(block_count, block_tokens, HD)

    def one_block(current, inputs):
        key_rows, value_rows, offset = inputs
        block_begin = offset * block_tokens
        key_segment = lax.dynamic_slice_in_dim(segment_all, block_begin, block_tokens, 0)
        skipped = jnp.logical_or(
            block_begin > last_query, key_segment[block_tokens - 1] < first_segment
        )

        def compute(previous):
            running_max, running_sum, running_acc = previous
            key_index = block_begin + jnp.arange(block_tokens, dtype=jnp.int32)
            allowed = (key_segment[None, :] == segment_own[:, None]) & (
                key_index[None, :] <= token_index[:, None]
            )
            scores = (
                jnp.einsum("qhd,kd->hqk", queries, key_rows, preferred_element_type=jnp.float32)
                * score_scale
            )
            scores = jnp.where(allowed[None], scores, masked_out)
            new_max = jnp.maximum(running_max, jnp.max(scores, axis=2))
            weights = jnp.where(allowed[None], jnp.exp(scores - new_max[..., None]), 0.0)
            factor = jnp.exp(running_max - new_max)
            new_sum = running_sum * factor + jnp.sum(weights, axis=2)
            update = jnp.einsum(
                "hqk,kd->hqd",
                weights.astype(jnp.bfloat16),
                value_rows,
                preferred_element_type=jnp.float32,
            )
            return (new_max, new_sum, running_acc * factor[..., None] + update)

        return (lax.cond(skipped, lambda previous: previous, compute, current), None)

    offsets = jnp.arange(block_count, dtype=jnp.int32)
    result, unused = lax.scan(one_block, initial, (key_blocks, value_blocks, offsets))
    final_max, final_sum, final_acc = result
    attention = (
        (final_acc / final_sum[..., None])
        .transpose(1, 0, 2)
        .reshape(block_tokens, query_cols)
        .astype(jnp.bfloat16)
    )
    pages_dev = PAGES_DEV
    page_len = block_tokens // pages_dev
    width_cols = cache_cols.shape[1]
    my_pages = cache_cols.reshape(pages_dev, page_len * width_cols)
    capacity = max(1, pages_dev // count_gy)
    slots_all = count_gy * capacity
    owners = (cache_slot // pages_dev).reshape(count_gy, pages_dev)
    page_range = jnp.arange(pages_dev, dtype=jnp.int32)
    earlier = page_range[None, :] < page_range[:, None]
    same_owner = owners[:, :, None] == owners[:, None, :]
    ranks = jnp.sum((same_owner & earlier[None]).astype(jnp.int32), axis=2)
    my_owner = lax.dynamic_index_in_dim(owners, where_gy, 0, keepdims=False)
    my_rank = lax.dynamic_index_in_dim(ranks, where_gy, 0, keepdims=False)
    target = my_owner * capacity + my_rank
    slot_range = jnp.arange(slots_all, dtype=jnp.int32)
    send_map = (slot_range[:, None] == target[None, :]).astype(jnp.bfloat16)
    outgoing = jnp.dot(send_map, my_pages, preferred_element_type=jnp.float32).astype(jnp.bfloat16)
    incoming = lax.all_to_all(outgoing, "gy", split_axis=0, concat_axis=0, tiled=True)
    wanted = where_gy * pages_dev + page_range
    matches = cache_slot[None, :] == wanted[:, None]
    page_ids = jnp.arange(cache_slot.shape[0], dtype=jnp.int32)
    source_page = jnp.sum(jnp.where(matches, page_ids[None, :], 0), axis=1)
    source_rank = jnp.sum(jnp.where(matches, ranks.reshape(-1)[None, :], 0), axis=1)
    source_slot = source_page // pages_dev * capacity + source_rank
    take_map = (source_slot[:, None] == slot_range[None, :]).astype(jnp.bfloat16)
    cache_block = jnp.dot(take_map, incoming, preferred_element_type=jnp.float32)
    cache_block = cache_block.astype(jnp.bfloat16).reshape(pages_dev, page_len, width_cols)
    return (attention, cache_block)


def solution(mesh):
    return jax.shard_map(
        local,
        mesh=mesh,
        in_specs=(P("gx", "gy"), P("gy"), P("gx", "gy"), P(None, "gy"), P(), P()),
        out_specs=(P("gy", "gx"), P("gy", None, "gx")),
        check_vma=False,
    )
```

profile of v0, /device:TPU:208, one launch (start us, length us, event | category | flops | bytes accessed | tf_op | source)
XLA Modules:
  0.0 692.0 jit_solution(10577667807313542377)
XLA Ops:
  7.2 1.2 fusion.19
  8.4 58.9 %psum.7 = f32[1024]{0:T(1024)S(1)} all-reduce(f32[1024]{0:T(1024)S(1)} %fusion.19), channel_id=1, replica_groups=mesh['gx'=8,'gy'=32] {'gy'}, use_global_device_ids=true, to_apply=%region_1.2 | all-reduce | flops 1024 | bytes 8192 | tf_op jit(solution)/shard_map/psum | solution.py:57
  67.9 1.9 fusion.21
  69.9 38.3 %all-gather.5.cloned.1.call-done = bf16[8192,128]{1,0:T(8,128)(2,1)} async-done(((bf16[1024,128]{1,0:T(8,128)(2,1)}), bf16[8192,128]{1,0:T(8,128)(2,1)}) %all-gather.5.cloned.1.call-update) | async-done | bytes 2097168 | tf_op jit(solution)/shard_map/all_gather | solution.py:61
  108.2 13.3 %fusion.23 = f32[8192,768]{0,1:T(8,128)} fusion(bf16[8192,128]{1,0:T(8,128)(2,1)} %all-gather.5.cloned.1.call-done, bf16[256,128]{1,0:T(8,128)(2,1)S(1)} %constant_dynamic-slice_fusion, bf16[512,128]{1,0:T(8,128)(2,1)} %param.12), kind=kOutput, calls=%fused_computation.42 | convolution fusion | flops 1611005952 | bytes 27459584 | tf_op jit(solution)/shard_map/dot_general | solution.py:64
  122.8 264.6 %reduce-scatter.2.cloned.1.call-done = f32[256,768]{0,1:T(8,128)} async-done(((f32[8192,768]{0,1:T(8,128)}), f32[256,768]{0,1:T(8,128)}) %reduce-scatter.2.cloned.1.call-update) | async-done | bytes 786448 | tf_op jit(solution)/shard_map/reduce_scatter | solution.py:63
  388.8 1.5 bitcast_select_fusion
  395.8 10.1 %all-to-all-start = ((bf16[32,2,1024]{2,1,0:T(2,128)(2,1)}), bf16[32,2,1024]{2,1,0:T(2,128)(2,1)S(1)}, u32[]{:S(2)}, u32[]{:S(2)}) async-start(bf16[32,2,1024]{2,1,0:T(2,128)(2,1)} %reshape.266), calls=%async_computation.1 | async-start | bytes 262144 | tf_op jit(solution)/shard_map/all_to_all | solution.py:157
  406.2 5.9 all-to-all-done
  413.1 52.7 %all-gather.7.cloned.1.call-done = bf16[8192,128]{0,1:T(8,128)(2,1)} async-done(((bf16[256,128]{0,1:T(8,128)(2,1)}), bf16[8192,128]{0,1:T(8,128)(2,1)}) %all-gather.7.cloned.1.call-update) | async-done | bytes 2097168 | tf_op jit(solution)/shard_map/all_gather | solution.py:93
  465.7 3.2 copy.72
  469.0 72.9 %all-gather.9.cloned.1.call-done = bf16[8192,1,128]{0,2,1:T(8,128)(2,1)} async-done(((bf16[256,1,128]{0,2,1:T(8,128)(2,1)}), bf16[8192,1,128]{0,2,1:T(8,128)(2,1)}) %all-gather.9.cloned.1.call-update) | async-done | bytes 2097168 | tf_op jit(solution)/shard_map/all_gather | solution.py:92
  541.8 4.1 copy.71
  546.0 138.6 %while.15 = (s32[]{:T(128)}, f32[4,256]{1,0:T(4,128)S(1)}, f32[4,256]{1,0:T(4,128)S(1)}, f32[4,256,128]{2,1,0:T(8,128)S(1)}, s32[32]{0:T(128)S(1)}, /*index=5*/s...) while((s32[]{:T(128)}, f32[4,256]{1,0:T(4,128)S(1)}, ...), condition=%wide.region_11.12_spmd.clone, body=%wide.region_6.11_spmd.clone.sunk | while | flops 137038352 | bytes 4926361 | solution.py:132
  568.6 2.1 conditional.3
  573.9 2.1 conditional.3
  574.0 1.2 fusion.46
  579.2 2.1 conditional.3
  584.5 2.1 conditional.3
  589.8 2.1 conditional.3
  595.1 2.1 conditional.3
  600.4 2.1 conditional.3
  605.7 2.1 conditional.3
  611.0 2.1 conditional.3
  616.3 2.1 conditional.3
  621.6 2.1 conditional.3
  626.9 2.1 conditional.3
  632.2 2.1 conditional.3
  637.5 2.1 conditional.3
  642.8 2.1 conditional.3
  648.1 2.1 conditional.3
  653.4 2.1 conditional.3
  (369 shorter events, 85.2 us)
Async XLA Ops:
  7.2 62.7 %copy-start = (bf16[1024,128]{1,0:T(8,128)(2,1)S(1)}, bf16[1024,128]{1,0:T(8,128)(2,1)}, u32[]{:S(2)}) copy-start(bf16[1024,128]{1,0:T(8,128)(2,1)} %param.13) | copy-start | bytes 786436
  7.2 101.1 %all-gather.5.cloned.1.call-start = ((), (), s32[]{:S(2)}) async-start(), calls=%async_computation.2 | async-start | bytes 2359296 | tf_op jit(solution)/shard_map/all_gather | solution.py:61
  69.8 317.6 %reduce-scatter.2.cloned.1.call-start = ((), (), s32[]{:S(2)}) async-start(), calls=%async_computation.3 | async-start | bytes 25952256 | tf_op jit(solution)/shard_map/reduce_scatter | solution.py:63
  121.6 0.7 copy-start.2
  121.6 270.1 %copy-start.1 = (s32[512]{0:T(512)S(1)}, s32[512]{0:T(512)}, u32[]{:S(2)}) copy-start(s32[512]{0:T(512)} %param.15) | copy-start | bytes 6148
  121.6 344.1 %all-gather.7.cloned.1.call-start = ((), (), s32[]{:S(2)}) async-start(), calls=%async_computation.4 | async-start | bytes 2162688 | tf_op jit(solution)/shard_map/all_gather | solution.py:93
  387.5 5.6 slice-start
  390.3 151.5 %all-gather.9.cloned.1.call-start = ((), (), s32[]{:S(2)}) async-start(), calls=%async_computation.5 | async-start | bytes 2162688 | tf_op jit(solution)/shard_map/all_gather | solution.py:92
  395.8 16.3 %all-to-all-start = ((bf16[32,2,1024]{2,1,0:T(2,128)(2,1)}), bf16[32,2,1024]{2,1,0:T(2,128)(2,1)S(1)}, u32[]{:S(2)}, u32[]{:S(2)}) async-start(bf16[32,2,1024]{2,1,0:T(2,128)(2,1)} %reshape.266), calls=%async_computation.1 | async-start | bytes 262144 | tf_op jit(solution)/shard_map/all_to_all | solution.py:157
Sparse Core Ops, SparseCore 0:
  69.9 38.2 all-gather.4
  121.7 265.7 reduce-scatter.1
  390.5 75.2 all-gather.6
  468.1 73.7 all-gather.8
where the time goes:
time: 694 us; the launch traced here: 692 us
  waiting for transfers between devices  434 us (63%)
  loops' own time  63.5 us (9%)
  blocking collectives  58.9 us (8%)
  local copies, waits for them, and re-layouts  52.8 us (8%)
  matrix products  42.2 us (6%)
  other arithmetic  16 us (2%)
  between operations  14 us (2%)
  starting transfers between devices  10.3 us (1%)
    reduce_scatter x1, waiting for transfers between devices, local(): lax.psum_scatter(lax.dot_general(gathered, stacked, contract, preferred_e...  265 us
    all_gather x1, waiting for transfers between devices, local(): key_piece = lax.all_gather(keys, 'gy', axis=0, tiled=True)  72.9 us
    another operation x1, loops' own time, local(): lax.scan(one_block, initial, (key_blocks, value_blocks, offsets))  62.1 us
    psum x1, blocking collectives, local(): totals = lax.psum(squares, 'gy')  58.9 us
    all_gather x1, waiting for transfers between devices, local(): value_piece = lax.all_gather(values, 'gy', axis=0, tiled=True)  52.7 us
    all_gather x1, waiting for transfers between devices, local(): gathered = lax.all_gather(normed, 'gx', axis=0, tiled=True)  38.3 us
    dot_general x17, matrix products, compute(): jnp.einsum('qhd,kd->hqk', queries, key_rows, preferred_element_type=jnp.f...  19.9 us
    slice x32, local copies, waits for them, and re-layouts, one_block(): key_segment[block_tokens - 1] < first_segment  18.9 us
  transfers between devices with their start and end apart: 5, of which 5 were waited for; matrix products, arithmetic and copies ran while one was open for 1% of the time, Pallas kernels for 0%

commit v1 on v0

--- a/solution.py
+++ b/solution.py
@@ -89,7 +89,9 @@
         jnp.zeros((heads_here, block_tokens), jnp.float32),
         jnp.zeros((heads_here, block_tokens, HD), jnp.float32),
     )
-    key_piece = lax.all_gather(keys, "gy", axis=0, tiled=True)
+    key_piece = jnp.concatenate(
+        lax.all_to_all(jnp.stack([keys] * lax.axis_size("gy")), "gy", 0, 0), axis=0
+    )
     value_piece = lax.all_gather(values, "gy", axis=0, tiled=True)
     block_count = key_piece.shape[0] // block_tokens
     key_blocks = key_piece.reshape(block_count, block_tokens, HD)

time: 694 us -> 645 us (0.929)
  waiting for transfers between devices: 434 us -> 376 us
  starting transfers between devices: 10.3 us -> 19.4 us
    all_gather x1 -> x0, waiting for transfers between devices: 72.9 us -> none  [local(): key_piece = lax.all_gather(keys, 'gy', axis=0, tiled=True)]
    all_gather x1, waiting for transfers between devices: 52.7 us -> 68.2 us  [local(): value_piece = lax.all_gather(values, 'gy', axis=0, tiled=True)]
    all_to_all x0 -> x1, starting transfers between devices: none -> 9.18 us  [local(): lax.all_to_all(jnp.stack([keys] * lax.axis_size('gy')), 'gy', 0, 0)]
  transfers between devices with their start and end apart: 5 -> 5, of which waited for: 5 -> 4; matrix products, arithmetic and copies ran while one was open for 1% -> 1% of each run, Pallas kernels for 0% -> 0%
where the time goes in v1:
time: 645 us; the launch traced here: 642 us
  waiting for transfers between devices  376 us (58%)
  loops' own time  64.5 us (10%)
  blocking collectives  58.9 us (9%)
  local copies, waits for them, and re-layouts  51.6 us (8%)
  matrix products  42.2 us (7%)
  starting transfers between devices  19.4 us (3%)
  other arithmetic  15.4 us (2%)
  between operations  14 us (2%)
    reduce_scatter x1, waiting for transfers between devices, local(): lax.psum_scatter(lax.dot_general(gathered, stacked, contract, preferred_e...  264 us
    all_gather x1, waiting for transfers between devices, local(): value_piece = lax.all_gather(values, 'gy', axis=0, tiled=True)  68.2 us
    another operation x1, loops' own time, local(): lax.scan(one_block, initial, (key_blocks, value_blocks, offsets))  63.1 us
    psum x1, blocking collectives, local(): totals = lax.psum(squares, 'gy')  58.9 us
    all_gather x1, waiting for transfers between devices, local(): gathered = lax.all_gather(normed, 'gx', axis=0, tiled=True)  38.3 us
    dot_general x17, matrix products, compute(): jnp.einsum('qhd,kd->hqk', queries, key_rows, preferred_element_type=jnp.f...  19.9 us
    dynamic_slice x32, local copies, waits for them, and re-layouts, local(): lax.scan(one_block, initial, (key_blocks, value_blocks, offsets))  19.8 us
    slice x32, local copies, waits for them, and re-layouts, one_block(): key_segment[block_tokens - 1] < first_segment  18.9 us
  transfers between devices with their start and end apart: 5, of which 4 were waited for; matrix products, arithmetic and copies ran while one was open for 1% of the time, Pallas kernels for 0%

profile of v1, /device:TPU:208, one launch (start us, length us, event | category | flops | bytes accessed | tf_op | source)
XLA Modules:
  0.0 642.4 jit_solution(6042787409294771400)
XLA Ops:
  7.2 1.2 fusion.19
  8.4 58.9 %psum.7 = f32[1024]{0:T(1024)S(1)} all-reduce(f32[1024]{0:T(1024)S(1)} %fusion.19), channel_id=1, replica_groups=mesh['gx'=8,'gy'=32] {'gy'}, use_global_device_ids=true, to_apply=%region_1.2 | all-reduce | flops 1024 | bytes 8192 | tf_op jit(solution)/shard_map/psum | solution.py:57
  67.9 1.9 fusion.21
  69.9 38.3 %all-gather.3.cloned.1.call-done = bf16[8192,128]{1,0:T(8,128)(2,1)} async-done(((bf16[1024,128]{1,0:T(8,128)(2,1)}), bf16[8192,128]{1,0:T(8,128)(2,1)}) %all-gather.3.cloned.1.call-update) | async-done | bytes 2097168 | tf_op jit(solution)/shard_map/all_gather | solution.py:61
  108.2 13.3 %fusion.23 = f32[8192,768]{0,1:T(8,128)} fusion(bf16[8192,128]{1,0:T(8,128)(2,1)} %all-gather.3.cloned.1.call-done, bf16[256,128]{1,0:T(8,128)(2,1)S(1)} %constant_dynamic-slice_fusion, bf16[512,128]{1,0:T(8,128)(2,1)} %param.12), kind=kOutput, calls=%fused_computation.42 | convolution fusion | flops 1611005952 | bytes 27459584 | tf_op jit(solution)/shard_map/dot_general | solution.py:64
  123.3 264.1 %reduce-scatter.2.cloned.1.call-done = f32[256,768]{0,1:T(8,128)} async-done(((f32[8192,768]{0,1:T(8,128)}), f32[256,768]{0,1:T(8,128)}) %reduce-scatter.2.cloned.1.call-update) | async-done | bytes 786448 | tf_op jit(solution)/shard_map/reduce_scatter | solution.py:63
  388.7 1.5 broadcast_select_fusion
  392.5 10.1 %all-to-all-start.1 = ((bf16[32,2,1024]{2,1,0:T(2,128)(2,1)}), bf16[32,2,1024]{2,1,0:T(2,128)(2,1)S(1)}, u32[]{:S(2)}, u32[]{:S(2)}) async-start(bf16[32,2,1024]{2,1,0:T(2,128)(2,1)} %reshape.263), calls=%async_computation.2 | async-start | bytes 262144 | tf_op jit(solution)/shard_map/all_to_all | solution.py:159
  403.5 5.1 all-to-all-done.1
  408.6 1.8 stack.2
  410.4 9.2 %all-to-all-start = ((bf16[32,256,128]{2,1,0:T(8,128)(2,1)}), bf16[32,256,128]{2,1,0:T(8,128)(2,1)}, u32[]{:S(2)}, u32[]{:S(2)}) async-start(bf16[32,256,128]{2,1,0:T(8,128)(2,1)} %stack.2), calls=%async_computation.1 | async-start | bytes 4194304 | tf_op jit(solution)/shard_map/all_to_all | solution.py:93
  422.9 68.2 %all-gather.5.cloned.1.call-done = bf16[8192,128]{0,1:T(8,128)(2,1)} async-done(((bf16[256,128]{0,1:T(8,128)(2,1)}), bf16[8192,128]{0,1:T(8,128)(2,1)}) %all-gather.5.cloned.1.call-update) | async-done | bytes 2097168 | tf_op jit(solution)/shard_map/all_gather | solution.py:95
  491.1 3.2 copy.71
  494.4 140.6 %while.15 = (s32[]{:T(128)}, f32[4,256]{1,0:T(4,128)S(1)}, f32[4,256]{1,0:T(4,128)S(1)}, f32[4,256,128]{2,1,0:T(8,128)S(1)}, s32[32]{0:T(128)S(1)}, /*index=5*/s...) while((s32[]{:T(128)}, f32[4,256]{1,0:T(4,128)S(1)}, ...), condition=%wide.region_11.12_spmd.clone, body=%wide.region_6.11_spmd.clone.sunk | while | flops 137038352 | bytes 4926361 | solution.py:134
  517.4 2.1 conditional.3
  517.5 1.2 fusion.46
  522.7 2.1 conditional.3
  528.1 2.1 conditional.3
  533.5 2.1 conditional.3
  538.8 2.1 conditional.3
  544.2 2.1 conditional.3
  549.6 2.1 conditional.3
  554.9 2.1 conditional.3
  560.3 2.1 conditional.3
  565.6 2.1 conditional.3
  571.0 2.1 conditional.3
  576.4 2.1 conditional.3
  581.7 2.1 conditional.3
  587.1 2.1 conditional.3
  592.5 2.1 conditional.3
  597.8 2.1 conditional.3
  603.2 2.1 conditional.3
  (369 shorter events, 86.4 us)
Async XLA Ops:
  7.2 62.7 %copy-start = (bf16[1024,128]{1,0:T(8,128)(2,1)S(1)}, bf16[1024,128]{1,0:T(8,128)(2,1)}, u32[]{:S(2)}) copy-start(bf16[1024,128]{1,0:T(8,128)(2,1)} %param.13) | copy-start | bytes 786436
  7.2 101.1 %all-gather.3.cloned.1.call-start = ((), (), s32[]{:S(2)}) async-start(), calls=%async_computation.3 | async-start | bytes 2359296 | tf_op jit(solution)/shard_map/all_gather | solution.py:61
  69.8 317.6 %reduce-scatter.2.cloned.1.call-start = ((), (), s32[]{:S(2)}) async-start(), calls=%async_computation.4 | async-start | bytes 25952256 | tf_op jit(solution)/shard_map/reduce_scatter | solution.py:63
  121.6 0.7 copy-start.2
  121.6 0.8 copy-start.1
  392.5 16.1 %all-to-all-start.1 = ((bf16[32,2,1024]{2,1,0:T(2,128)(2,1)}), bf16[32,2,1024]{2,1,0:T(2,128)(2,1)S(1)}, u32[]{:S(2)}, u32[]{:S(2)}) async-start(bf16[32,2,1024]{2,1,0:T(2,128)(2,1)} %reshape.263), calls=%async_computation.2 | async-start | bytes 262144 | tf_op jit(solution)/shard_map/all_to_all | solution.py:159
  402.6 88.4 %all-gather.5.cloned.1.call-start = ((), (), s32[]{:S(2)}) async-start(), calls=%async_computation.5 | async-start | bytes 2162688 | tf_op jit(solution)/shard_map/all_gather | solution.py:95
  410.4 10.8 %slice-start = ((f32[256,768]{0,1:T(8,128)}), f32[256,512]{0,1:T(8,128)S(1)}, s32[]{:S(2)}) async-start(f32[256,768]{0,1:T(8,128)} %reduce-scatter.2.cloned.1.call-done), calls=%async_computation.6 | async-start | bytes 1048576 | tf_op jit(solution)/shard_map/slice | solution.py:77
  410.4 83.9 %all-to-all-start = ((bf16[32,256,128]{2,1,0:T(8,128)(2,1)}), bf16[32,256,128]{2,1,0:T(8,128)(2,1)}, u32[]{:S(2)}, u32[]{:S(2)}) async-start(bf16[32,256,128]{2,1,0:T(8,128)(2,1)} %stack.2), calls=%async_computation.1 | async-start | bytes 4194304 | tf_op jit(solution)/shard_map/all_to_all | solution.py:93
Sparse Core Ops, SparseCore 0:
  69.9 38.2 all-gather.2
  121.7 265.7 reduce-scatter.1
  405.9 85.0 all-gather.4
